TPU v7x, 128 devices: a whole 4x4x4 slice. The times are simulated.
128 devices in a mesh: row: 8 (over z, core), col: 16 (over y, x).
Axes of the slice: x: 4, y: 4, z: 4, core: 2. Of those that a mesh axis runs over, the one named last changes fastest.
Arguments:
- psi_val: float32 [64, 128, 128, 128], P(None, 'row', 'col'), may hold values from -6 to 6
- psi_cond: float32 [64, 128, 128, 128], P(None, 'row', 'col'), may hold values from -6 to 6
- eps_val: float32 [64], replicated, may hold values from -12 to -1
- eps_cond: float32 [64], replicated, may hold values from 1 to 12
- val_index: int32 [128], replicated, may hold values from 0 to 63
- cond_index: int32 [128], replicated, may hold values from 0 to 63
- gmap: int32 [8192], replicated, may hold values from 0 to 2097151, as said below
- chi0_in: float32 [2, 8192, 8192], P(None, 'row', 'col'), may hold values from -6 to 6
Outputs:
- chi0_out: float32 [2, 8192, 8192], P(None, 'row', 'col')
Inputs may be any that keep to these rules, and one draw needn't show every extreme that they name: gmap holds 8192 distinct entries. Entries g of device block d = g // 64 (d = r * 16 + c) have ky in [r * 16, (r + 1) * 16) and kz in [c * 8, (c + 1) * 8); kx is any.
All inputs are finite; a program needn't handle non-finite values.
Results may differ from a plain program's by a relative error of at most 0.000068.
Values sent between devices are 32-bit elements; how exact they have to be, the bound alone decides.
No kernel may reach another device: no remote copies, remote signals or barrier semaphores. Data moves between devices by JAX's collectives and lax.ppermute only.
A program may use at most 128 MiB of HBM per device.

v0:
```python
import math

import jax
import numpy as np
import jax.numpy as jnp
from jax import lax
from jax.sharding import PartitionSpec as P

GRID = 128
NG = 8192


HIGH = lax.Precision.HIGHEST


def phase_table(left, right, length):
    phase = left[:, None] * right[None, :] % length
    angle = phase.astype(jnp.float32) * (2.0 * math.pi / length)
    return (jnp.cos(angle), jnp.sin(angle))


def contract_pairs(left, right):
    return lax.dot_general(
        left, right, (((1,), (1,)), ((), ())), precision=HIGH, preferred_element_type=jnp.float32
    )


def on_device(psi_val, psi_cond, eps_val, eps_cond, val_index, cond_index, gmap, chi0_in):
    pairs = val_index.shape[0]
    scale = 1.0 / math.sqrt(GRID**3)
    row_pos = lax.axis_index("row")
    col_pos = lax.axis_index("col")
    mesh_cols = lax.axis_size("col")
    mesh_rows = lax.axis_size("row")
    per_device = NG // (mesh_rows * mesh_cols)
    row_span = GRID // mesh_rows
    col_span = GRID // mesh_cols
    steps = jnp.arange(GRID, dtype=jnp.int32)

    mirror = mesh_cols - 1 - col_pos
    low = jnp.minimum(col_pos, mirror)
    side = col_pos // (mesh_cols // 2)
    span_z = col_span + 1
    x_half = row_span // 2
    by_block = gmap.reshape(mesh_rows, mesh_cols, per_device)
    direct = lax.dynamic_index_in_dim(by_block, low, axis=1, keepdims=False)
    mirrored = lax.dynamic_index_in_dim(by_block, mesh_cols - 1 - low, axis=1, keepdims=False)
    both = jnp.stack([direct, mirrored], axis=1).reshape(-1)
    flip = (jnp.arange(both.shape[0], dtype=jnp.int32) // per_device) % 2
    freq_x = both // (GRID * GRID)
    freq_y = both // GRID % GRID
    freq_z = both % GRID
    freq_x = jnp.where(flip == 1, (GRID - freq_x) % GRID, freq_x)
    freq_y = jnp.where(flip == 1, (GRID - freq_y) % GRID, freq_y)
    freq_z = jnp.where(flip == 1, (GRID - freq_z) % GRID, freq_z) - low * col_span
    sign = jnp.where(flip == 1, -1.0, 1.0).astype(jnp.float32)
    pick = freq_y * span_z + freq_z
    x_glob = row_pos * row_span + side * x_half + jnp.arange(x_half, dtype=jnp.int32)
    cos_x, sin_x = phase_table(x_glob, freq_x, GRID)

    kz_set = (jnp.arange(mesh_cols // 2, dtype=jnp.int32)[:, None] * col_span
              + jnp.arange(span_z, dtype=jnp.int32)[None, :]).reshape(-1)
    cos_z, sin_z = phase_table(steps, kz_set, GRID)
    table_z = jnp.stack([cos_z, -sin_z], axis=-1).reshape(GRID, mesh_cols // 2, span_z, 2)
    table_z = jnp.stack([table_z, table_z[:, ::-1]], axis=0)
    cos_y, sin_y = phase_table(steps, steps, GRID)
    table_y = jnp.stack(
        [jnp.stack([cos_y, -sin_y], axis=-1), jnp.stack([sin_y, cos_y], axis=-1)], axis=1
    ).reshape(mesh_cols, col_span, 2, GRID, 2)

    chunks = 2
    chunk = x_half // chunks
    pieces = []
    for i in range(chunks):
        lo = slice(i * chunk, (i + 1) * chunk)
        hi = slice(x_half + i * chunk, x_half + (i + 1) * chunk)
        band_v = jnp.stack([psi_val[:, lo], psi_val[:, hi]], axis=1)
        band_c = jnp.stack([psi_cond[:, lo], psi_cond[:, hi]], axis=1)
        rho = jnp.take(band_v, val_index, axis=0) * jnp.take(band_c, cond_index, axis=0)
        z_all = jnp.einsum("phxyz,hzcjt->hcpxyjt", rho, table_z, precision=HIGH)
        z_all = z_all.reshape((mesh_cols,) + z_all.shape[2:])
        if i >= 2:
            z_all, pieces[i - 2] = lax.optimization_barrier((z_all, pieces[i - 2]))
        z_mine = lax.all_to_all(z_all, "col", split_axis=0, concat_axis=0, tiled=True)
        y_all = jnp.einsum("spxyjt,syteu->ejuxp", z_mine, table_y, precision=HIGH)
        flat = y_all.reshape(GRID * span_z, 2, chunk, pairs)
        chosen = jnp.take(flat, pick, axis=0)
        c_re = chosen[:, 0]
        c_im = chosen[:, 1]
        cx = cos_x[lo].T[:, :, None]
        sx = sin_x[lo].T[:, :, None]
        part_re = jnp.sum(c_re * cx + c_im * sx, axis=1)
        part_im = jnp.sum(c_im * cx - c_re * sx, axis=1)
        pieces.append(jnp.stack([part_re, part_im], axis=1))
    partial = pieces[0]
    for piece in pieces[1:]:
        partial = partial + piece
    partial = partial * jnp.stack([jnp.ones_like(sign), sign], axis=1)[:, :, None] * scale
    block = 2 * per_device
    spread = partial.reshape(mesh_rows, block, 2, pairs)
    gathered = lax.all_to_all(spread, "row", split_axis=0, concat_axis=0, tiled=True)
    both_blocks = jnp.sum(gathered, axis=0).reshape(2, per_device, 2, pairs)
    mine = lax.dynamic_index_in_dim(both_blocks, side, axis=0, keepdims=False)
    theirs = lax.dynamic_index_in_dim(both_blocks, 1 - side, axis=0, keepdims=False)
    partner = lax.ppermute(theirs, "col", [(c, mesh_cols - 1 - c) for c in range(mesh_cols)])
    own = mine + partner
    copies = jnp.broadcast_to(own[None], (mesh_cols,) + own.shape)
    row_blocks = lax.all_to_all(copies, "col", split_axis=0, concat_axis=0, tiled=True)
    rows = row_blocks.reshape(mesh_cols * per_device, 2, pairs)
    half = mesh_cols // 2
    send = lax.dynamic_slice_in_dim(rows, (col_pos // half) * half * per_device, half * per_device, 0)
    perm = []
    for src_r in range(mesh_rows):
        for src_c in range(mesh_cols):
            dst_r = src_c % half
            dst_c = 2 * src_r + src_c // half
            perm.append((src_r * mesh_cols + src_c, dst_r * mesh_cols + dst_c))
    cols = lax.ppermute(send, ("row", "col"), perm)

    val_hot = val_index[:, None] == jnp.arange(eps_val.shape[0], dtype=jnp.int32)[None, :]
    cond_hot = cond_index[:, None] == jnp.arange(eps_cond.shape[0], dtype=jnp.int32)[None, :]
    energy_v = jnp.sum(jnp.where(val_hot, eps_val[None, :], 0.0), axis=1)
    energy_c = jnp.sum(jnp.where(cond_hot, eps_cond[None, :], 0.0), axis=1)
    weight = (-6.0 / (math.sqrt(pairs) * (energy_c - energy_v)))[None, :]
    rows_re = rows[:, 0]
    rows_im = rows[:, 1]
    cols_re = cols[:, 0]
    cols_im = cols[:, 1]
    out_re = (
        chi0_in[0]
        + contract_pairs(weight * rows_re, cols_re)
        + contract_pairs(weight * rows_im, cols_im)
    )
    out_im = (
        chi0_in[1]
        + contract_pairs(weight * rows_im, cols_re)
        - contract_pairs(weight * rows_re, cols_im)
    )
    return jnp.stack([out_re, out_im])


def solution(mesh):
    return jax.shard_map(
        on_device,
        mesh=mesh,
        in_specs=(
            P(None, "row", "col", None),
            P(None, "row", "col", None),
            P(),
            P(),
            P(),
            P(),
            P(),
            P(None, "row", "col"),
        ),
        out_specs=P(None, "row", "col"),
        check_vma=False,
    )
```

profile of v0, /device:TPU:24, one launch (start us, length us, event | category | flops | bytes accessed | tf_op | source)
XLA Modules:
  0.0 367.5 jit_solution(6099268640693206655)
XLA Ops:
  0.0 0.7 compare_select_fusion.4
  0.7 0.7 compare_and_fusion.1
  1.4 0.3 fusion.47
  1.8 0.3 fusion.48
  2.1 2.6 slice_bitcast_fusion.7
  4.8 1.8 pad_maximum_fusion.1
  6.5 4.4 %gather_fusion = f32[128,2,4,8,128]{4,3,2,1,0:T(8,128)} fusion(f32[64,2,4,8,128]{4,3,2,0,1:T(8,128)} %get-tuple-element.52, s32[1024]{0:T(1024)S(1)} %pad_clamp_fusion.1), kind=kCustom, calls=%fused_computation.clone | custom fusion | bytes 8389120 | tf_op jit(solution)/shard_map/jit(_take)/gather | solution.py:79
  10.9 2.8 gather_fusion.3
  13.7 2.6 slice_bitcast_fusion.5
  16.4 2.0 pad_maximum_fusion.2
  18.4 4.4 %gather_fusion.4 = f32[128,2,4,8,128]{4,3,2,1,0:T(8,128)} fusion(f32[64,2,4,8,128]{4,3,2,0,1:T(8,128)} %get-tuple-element.47, s32[1024]{0:T(1024)S(1)} %pad_clamp_fusion), kind=kCustom, calls=%fused_computation.4.clone | custom fusion | bytes 8389120 | tf_op jit(solution)/shard_map/jit(_take)/gather | solution.py:79
  22.8 2.8 gather_fusion.1
  25.6 8.8 %fusion.10 = (f32[128,2,4,8,128,1,1]{4,3,2,1,0,6,5:T(8,128)}, f32[128,2,4,8,128,1,1]{4,3,2,1,0,6,5:T(8,128)S(1)}) fusion(f32[128,2,4,8,128]{4,3,2,1,0:T(8,128)} %gather_fusion.4, f32[128,2,4,8,128]{4,3,2,1,0:T(8,128)} %gather_fusion.3, pred[128]{0:T(512)(128)(4,1)S(1)} %get-tuple-element.50, pred[128]{0:T(512)(128)(4,1)S(1)} %get-tuple-element.51, ...), kind=kLoop, calls=%fused_computation.18 | loop fusion | flops 6291456 | bytes 25166080 | tf_op jit(solution)/shard_map/mul | solution.py:79
  34.4 9.0 %fusion.8 = f32[2,8,9,2,128,4,8]{4,2,6,5,3,1,0:T(8,128)S(1)} fusion(f32[128,2,4,8,128,1,1]{4,3,2,1,0,6,5:T(8,128)S(1)} %get-tuple-element.45, f32[1,128,8,9,2]{1,3,4,2,0:T(8,128)S(1)} %reverse_bitcast_fusion, f32[1,128,8,9,1]{1,3,4,2,0:T(8,128)S(1)} %get-tuple-element.39, f32[1,128,8,9,1]{1,3,4,2,0:T(8,128)S(1)} %get-tuple-element.38), kind=kOutput, calls=%fused_computation.15 | convolution fusion | flops 1812013056 | bytes 9060352 | tf_op jit(solution)/shard_map/phxyz,hzcjt->hcpxyjt/dot_general | solution.py:80
  43.4 4.4 %copy.70 = f32[16,128,4,8,9,2]{1,3,5,4,2,0:T(8,128)} copy(f32[16,128,4,8,9,2]{1,4,3,2,5,0:T(8,128)S(1)} %bitcast.145) | data formatting | bytes 9437184 | tf_op jit(solution)/shard_map/reshape | solution.py:81
  47.9 7.2 %all-to-all-start = ((f32[16,128,4,8,9,2]{1,3,5,4,2,0:T(8,128)}), f32[16,128,4,8,9,2]{1,3,5,4,2,0:T(8,128)}, u32[]{:S(2)}, u32[]{:S(2)}) async-start(f32[16,128,4,8,9,2]{1,3,5,4,2,0:T(8,128)} %copy.70), calls=%async_computation | async-start | bytes 9437184 | tf_op jit(solution)/shard_map/all_to_all | solution.py:84
  55.0 11.4 %fusion.6 = f32[2,8,9,2,128,4,8]{4,2,6,5,3,1,0:T(8,128)S(1)} fusion(f32[128,2,4,8,128,1,1]{4,3,2,1,0,6,5:T(8,128)} %get-tuple-element.44, f32[1,128,8,9,2]{1,3,4,2,0:T(8,128)S(1)} %reverse_bitcast_fusion, f32[1,128,8,9,1]{1,3,4,2,0:T(8,128)S(1)} %get-tuple-element.39, f32[1,128,8,9,1]{1,3,4,2,0:T(8,128)S(1)} %get-tuple-element.38), kind=kOutput, calls=%fused_computation.13 | convolution fusion | flops 1812013056 | bytes 9060352 | tf_op jit(solution)/shard_map/phxyz,hzcjt->hcpxyjt/dot_general | solution.py:80
  66.4 4.3 %copy.75 = f32[16,128,4,8,9,2]{1,3,5,4,2,0:T(8,128)} copy(f32[16,128,4,8,9,2]{1,4,3,2,5,0:T(8,128)S(1)} %bitcast.144) | data formatting | bytes 9437184 | tf_op jit(solution)/shard_map/reshape | solution.py:81
  70.8 53.9 %all-to-all-done = f32[16,128,4,8,9,2]{1,3,5,4,2,0:T(8,128)} async-done(((f32[16,128,4,8,9,2]{1,3,5,4,2,0:T(8,128)}), f32[16,128,4,8,9,2]{1,3,5,4,2,0:T(8,128)}, u32[]{:S(2)}, u32[]{:S(2)}) %all-to-all-start) | async-done | bytes 4718624 | tf_op jit(solution)/shard_map/all_to_all | solution.py:84
  124.7 6.7 %all-to-all-start.1 = ((f32[16,128,4,8,9,2]{1,3,5,4,2,0:T(8,128)}), f32[16,128,4,8,9,2]{1,3,5,4,2,0:T(8,128)}, u32[]{:S(2)}, u32[]{:S(2)}) async-start(f32[16,128,4,8,9,2]{1,3,5,4,2,0:T(8,128)} %copy.75), calls=%async_computation.1 | async-start | bytes 9437184 | tf_op jit(solution)/shard_map/all_to_all | solution.py:84
  132.1 2.1 fusion.28
  134.6 9.5 %fusion.12 = f32[128,9,2,4,128]{4,0,1,3,2:T(8,128)S(1)} fusion(f32[16,128,4,8,9,2]{1,3,5,4,2,0:T(8,128)} %all-to-all-done, f32[16,8,1,128,1]{3,0,1,2,4:T(8,128)S(1)} %get-tuple-element.37, f32[16,8,1,128,1]{3,0,1,2,4:T(8,128)S(1)} %get-tuple-element.36, f32[16,8,1,128,1]{3,0,1,2,4:T(8,128)S(1)} %get-tuple-element.35), kind=kOutput, calls=%fused_computation.21 | convolution fusion | flops 3624075264 | bytes 9633792 | tf_op jit(solution)/shard_map/spxyjt,syteu->ejuxp/dot_general | solution.py:85
  144.0 5.2 %copy.72 = f32[128,9,2,4,128]{4,3,2,1,0:T(4,128)} copy(f32[128,9,2,4,128]{4,0,1,3,2:T(8,128)S(1)} %fusion.12) | data formatting | bytes 9437184 | tf_op jit(solution)/shard_map/spxyjt,syteu->ejuxp/transpose | solution.py:85
  149.2 49.6 %all-to-all-done.1 = f32[16,128,4,8,9,2]{1,3,5,4,2,0:T(8,128)} async-done(((f32[16,128,4,8,9,2]{1,3,5,4,2,0:T(8,128)}), f32[16,128,4,8,9,2]{1,3,5,4,2,0:T(8,128)}, u32[]{:S(2)}, u32[]{:S(2)}) %all-to-all-start.1) | async-done | bytes 4718624 | tf_op jit(solution)/shard_map/all_to_all | solution.py:84
  198.8 9.6 %fusion.15 = f32[128,9,2,4,128]{4,0,1,3,2:T(8,128)S(1)} fusion(f32[16,128,4,8,9,2]{1,3,5,4,2,0:T(8,128)} %all-to-all-done.1, f32[16,8,1,128,1]{3,0,1,2,4:T(8,128)S(1)} %get-tuple-element.37, f32[16,8,1,128,1]{3,0,1,2,4:T(8,128)S(1)} %get-tuple-element.36, f32[16,8,1,128,1]{3,0,1,2,4:T(8,128)S(1)} %get-tuple-element.35), kind=kOutput, calls=%fused_computation.22 | convolution fusion | flops 3624075264 | bytes 9633792 | tf_op jit(solution)/shard_map/spxyjt,syteu->ejuxp/dot_general | solution.py:85
  208.5 5.2 %copy.77 = f32[128,9,2,4,128]{4,3,2,1,0:T(4,128)} copy(f32[128,9,2,4,128]{4,0,1,3,2:T(8,128)S(1)} %fusion.15) | data formatting | bytes 9437184 | tf_op jit(solution)/shard_map/spxyjt,syteu->ejuxp/transpose | solution.py:85
  213.6 12.0 %gather_fusion.2 = f32[1024,2,4,128]{3,2,1,0:T(4,128)} fusion(f32[1152,2,4,128]{3,2,1,0:T(4,128)} %bitcast.146, s32[1024]{0:T(1024)S(1)} %broadcast_clamp_fusion), kind=kCustom, calls=%fused_computation.1.clone | custom fusion | bytes 8392704 | tf_op jit(solution)/shard_map/jit(_take)/gather | solution.py:87
  225.6 11.8 %gather_fusion.5 = f32[1024,2,4,128]{3,2,1,0:T(4,128)} fusion(f32[1152,2,4,128]{3,2,1,0:T(4,128)} %bitcast.147, s32[1024]{0:T(1024)S(1)} %broadcast_clamp_fusion), kind=kCustom, calls=%fused_computation.5.clone | custom fusion | bytes 8392704 | tf_op jit(solution)/shard_map/jit(_take)/gather | solution.py:87
  237.4 6.0 %broadcast_select_fusion = (f32[1024,2,4,128]{3,2,1,0:T(4,128)S(1)}, f32[1024,2,4,128]{3,2,1,0:T(4,128)S(1)}) fusion(f32[1024,2,4,128]{3,2,1,0:T(4,128)} %gather_fusion.5, pred[1024]{0:T(1024)(128)(4,1)S(1)} %get-tuple-element.11, f32[1024,2,4,128]{3,2,1,0:T(4,128)} %gather_fusion.2), kind=kLoop, calls=%fused_computation.37 | loop fusion | flops 2097152 | bytes 16778240 | tf_op jit(solution)/shard_map/jit(_take)/select_n | solution.py:87
  243.5 6.3 %add_reduce_fusion = (f32[1024,128]{1,0:T(8,128)S(1)}, f32[1024,128]{1,0:T(8,128)S(1)}) fusion(f32[1024,2,4,128]{3,2,1,0:T(4,128)S(1)} %get-tuple-element.42, f32[1024,4]{1,0:T(8,128)S(1)} %get-tuple-element.29, f32[1024,4]{1,0:T(8,128)S(1)} %get-tuple-element.55), kind=kLoop, calls=%fused_computation.40 | loop fusion | flops 3932160 | bytes 5275648 | tf_op jit(solution)/shard_map/reduce_sum | solution.py:92
  249.8 6.3 %add_reduce_fusion.1 = (f32[1024,128]{1,0:T(8,128)S(1)}, f32[1024,128]{1,0:T(8,128)S(1)}) fusion(f32[1024,2,4,128]{3,2,1,0:T(4,128)S(1)} %get-tuple-element.43, f32[1024,4]{1,0:T(8,128)S(1)} %get-tuple-element.30, f32[1024,4]{1,0:T(8,128)S(1)} %get-tuple-element.54), kind=kLoop, calls=%fused_computation.42 | loop fusion | flops 3932160 | bytes 5275648 | tf_op jit(solution)/shard_map/reduce_sum | solution.py:92
  256.1 1.4 fusion.23
  257.5 5.5 %all-to-all-start.2 = ((f32[8,128,2,128]{3,1,2,0:T(8,128)}), f32[8,128,2,128]{3,1,2,0:T(8,128)S(1)}, u32[]{:S(2)}, u32[]{:S(2)}) async-start(f32[8,128,2,128]{3,1,2,0:T(8,128)} %fusion.23), calls=%async_computation.2 | async-start | bytes 2097152 | tf_op jit(solution)/shard_map/all_to_all | solution.py:101
  263.0 16.0 %all-to-all-done.2 = f32[8,128,2,128]{3,1,2,0:T(8,128)S(1)} async-done(((f32[8,128,2,128]{3,1,2,0:T(8,128)}), f32[8,128,2,128]{3,1,2,0:T(8,128)S(1)}, u32[]{:S(2)}, u32[]{:S(2)}) %all-to-all-start.2) | async-done | bytes 1048608 | tf_op jit(solution)/shard_map/all_to_all | solution.py:101
  279.0 1.1 collective-permute-start
  280.1 6.7 %collective-permute-done = f32[64,2,128]{2,0,1:T(8,128)S(1)} collective-permute-done((f32[64,2,128]{2,0,1:T(8,128)S(1)}, f32[64,2,128]{2,0,1:T(8,128)S(1)}, u32[]{:S(2)}, u32[]{:S(2)}) %collective-permute-start) | collective-permute-done | bytes 65568 | tf_op jit(solution)/shard_map/ppermute | solution.py:105
  287.0 1.4 broadcast_in_dim.74
  288.3 4.5 %all-to-all-start.3 = ((f32[16,64,2,128]{3,2,1,0:T(2,128)}), f32[16,64,2,128]{3,2,1,0:T(2,128)S(1)}, u32[]{:S(2)}, u32[]{:S(2)}) async-start(f32[16,64,2,128]{3,2,1,0:T(2,128)} %broadcast_in_dim.74), calls=%async_computation.3 | async-start | bytes 2097152 | tf_op jit(solution)/shard_map/all_to_all | solution.py:108
  292.9 13.6 %all-to-all-done.3 = f32[16,64,2,128]{3,2,1,0:T(2,128)S(1)} async-done(((f32[16,64,2,128]{3,2,1,0:T(2,128)}), f32[16,64,2,128]{3,2,1,0:T(2,128)S(1)}, u32[]{:S(2)}, u32[]{:S(2)}) %all-to-all-start.3) | async-done | bytes 1048608 | tf_op jit(solution)/shard_map/all_to_all | solution.py:108
  306.5 4.7 %collective-permute-start.1 = (f32[512,2,128]{2,1,0:T(2,128)S(1)}, f32[512,2,128]{2,1,0:T(2,128)S(1)}, u32[]{:S(2)}, u32[]{:S(2)}) collective-permute-start(f32[512,2,128]{2,1,0:T(2,128)S(1)} %constant_dynamic-slice_fusion), channel_id=1, source_target_pairs={{0,0},{1,16},{2,32},{3,48},{4,64},{5,80},{6,96},{7,112},{8,1},{9,1... | collective-permute-start | bytes 1572872 | tf_op jit(solution)/shard_map/ppermute | solution.py:118
  311.4 0.7 slice_multiply_fusion
  312.1 45.2 %collective-permute-done.1 = f32[512,2,128]{2,1,0:T(2,128)S(1)} collective-permute-done((f32[512,2,128]{2,1,0:T(2,128)S(1)}, f32[512,2,128]{2,1,0:T(2,128)S(1)}, u32[]{:S(2)}, u32[]{:S(2)}) %collective-permute-start.1) | collective-permute-done | bytes 524320 | tf_op jit(solution)/shard_map/ppermute | solution.py:118
  357.2 0.4 fusion.77
  357.7 1.8 fusion.79
  359.5 1.8 fusion.78
  361.3 1.8 fusion.80
  363.1 2.1 fusion.21
  365.2 2.0 copy-done.7
  (42 shorter events, 1.4 us)
Async XLA Ops:
  47.9 76.8 %all-to-all-start = ((f32[16,128,4,8,9,2]{1,3,5,4,2,0:T(8,128)}), f32[16,128,4,8,9,2]{1,3,5,4,2,0:T(8,128)}, u32[]{:S(2)}, u32[]{:S(2)}) async-start(f32[16,128,4,8,9,2]{1,3,5,4,2,0:T(8,128)} %copy.70), calls=%async_computation | async-start | bytes 9437184 | tf_op jit(solution)/shard_map/all_to_all | solution.py:84
  70.8 60.7 %copy-start.1 = (s32[8192]{0:T(1024)S(1)}, s32[8192]{0:T(1024)}, u32[]{:S(2)}) copy-start(s32[8192]{0:T(1024)} %param.18) | copy-start | bytes 98308
  124.7 74.1 %all-to-all-start.1 = ((f32[16,128,4,8,9,2]{1,3,5,4,2,0:T(8,128)}), f32[16,128,4,8,9,2]{1,3,5,4,2,0:T(8,128)}, u32[]{:S(2)}, u32[]{:S(2)}) async-start(f32[16,128,4,8,9,2]{1,3,5,4,2,0:T(8,128)} %copy.75), calls=%async_computation.1 | async-start | bytes 9437184 | tf_op jit(solution)/shard_map/all_to_all | solution.py:84
  257.5 53.7 %copy-start.2 = (s32[128]{0:T(128)S(1)}, s32[128]{0:T(128)}, u32[]{:S(2)}) copy-start(s32[128]{0:T(128)} %param.17) | copy-start | bytes 1540
  257.5 53.7 %copy-start.3 = (s32[128]{0:T(128)S(1)}, s32[128]{0:T(128)}, u32[]{:S(2)}) copy-start(s32[128]{0:T(128)} %param.16) | copy-start | bytes 1540
  257.5 53.7 %copy-start.4 = (f32[64]{0:T(128)S(1)}, f32[64]{0:T(128)}, u32[]{:S(2)}) copy-start(f32[64]{0:T(128)} %param.14) | copy-start | bytes 772
  257.5 53.7 %copy-start.5 = (f32[64]{0:T(128)S(1)}, f32[64]{0:T(128)}, u32[]{:S(2)}) copy-start(f32[64]{0:T(128)} %param.15) | copy-start | bytes 772
  257.5 21.4 %all-to-all-start.2 = ((f32[8,128,2,128]{3,1,2,0:T(8,128)}), f32[8,128,2,128]{3,1,2,0:T(8,128)S(1)}, u32[]{:S(2)}, u32[]{:S(2)}) async-start(f32[8,128,2,128]{3,1,2,0:T(8,128)} %fusion.23), calls=%async_computation.2 | async-start | bytes 2097152 | tf_op jit(solution)/shard_map/all_to_all | solution.py:101
  279.0 7.9 %collective-permute-start = (f32[64,2,128]{2,0,1:T(8,128)S(1)}, f32[64,2,128]{2,0,1:T(8,128)S(1)}, u32[]{:S(2)}, u32[]{:S(2)}) collective-permute-start(f32[64,2,128]{2,0,1:T(8,128)S(1)} %dynamic-slice_bitcast_fusion), channel_id=1, source_target_pairs={{0,15},{1,14},{2,13},{3,12},{4,11},{5,10},{6,9},{7,8},{8,7},{9,6},... | collective-permute-start | bytes 196616 | tf_op jit(solution)/shard_map/ppermute | solution.py:105
  288.3 18.1 %all-to-all-start.3 = ((f32[16,64,2,128]{3,2,1,0:T(2,128)}), f32[16,64,2,128]{3,2,1,0:T(2,128)S(1)}, u32[]{:S(2)}, u32[]{:S(2)}) async-start(f32[16,64,2,128]{3,2,1,0:T(2,128)} %broadcast_in_dim.74), calls=%async_computation.3 | async-start | bytes 2097152 | tf_op jit(solution)/shard_map/all_to_all | solution.py:108
  306.5 50.8 %collective-permute-start.1 = (f32[512,2,128]{2,1,0:T(2,128)S(1)}, f32[512,2,128]{2,1,0:T(2,128)S(1)}, u32[]{:S(2)}, u32[]{:S(2)}) collective-permute-start(f32[512,2,128]{2,1,0:T(2,128)S(1)} %constant_dynamic-slice_fusion), channel_id=1, source_target_pairs={{0,0},{1,16},{2,32},{3,48},{4,64},{5,80},{6,96},{7,112},{8,1},{9,1... | collective-permute-start | bytes 1572872 | tf_op jit(solution)/shard_map/ppermute | solution.py:118
  357.7 5.4 %copy-start = (f32[2,1024,512]{2,1,0:T(8,128)S(1)}, f32[2,1024,512]{2,1,0:T(8,128)}, u32[]{:S(2)}) copy-start(f32[2,1024,512]{2,1,0:T(8,128)} %param.19) | copy-start | bytes 12582916
  357.7 5.4 %copy-start.6 = (f32[2,1024,512]{2,1,0:T(8,128)S(1)}, f32[2,1024,512]{2,1,0:T(8,128)}, u32[]{:S(2)}) copy-start(f32[2,1024,512]{2,1,0:T(8,128)} %custom-call.12) | copy-start | bytes 12582916
  365.2 2.0 copy-start.7
where the time goes:
time: 371 us; the launch traced here: 367 us
  waiting for transfers between devices  185 us (50%)
  local copies, waits for them, and re-layouts  67 us (18%)
  matrix products  47 us (13%)
  other arithmetic  38.2 us (10%)
  starting transfers between devices  29.7 us (8%)
    all_to_all x2, waiting for transfers between devices, on_device(): lax.all_to_all(z_all, 'col', split_axis=0, concat_axis=0, tiled=True)  103 us
    ppermute x1, waiting for transfers between devices, on_device(): cols = lax.ppermute(send, ('row', 'col'), perm)  45.2 us
    gather x2, local copies, waits for them, and re-layouts, on_device(): chosen = jnp.take(flat, pick, axis=0)  23.8 us
    dot_general x2, matrix products, on_device(): z_all = jnp.einsum('phxyz,hzcjt->hcpxyjt', rho, table_z, precision=HIGH)  20.4 us
    dot_general x2, matrix products, on_device(): y_all = jnp.einsum('spxyjt,syteu->ejuxp', z_mine, table_y, precision=HIGH)  19.1 us
    all_to_all x1, waiting for transfers between devices, on_device(): lax.all_to_all(spread, 'row', split_axis=0, concat_axis=0, tiled=True)  16 us
    all_to_all x2, starting transfers between devices, on_device(): lax.all_to_all(z_all, 'col', split_axis=0, concat_axis=0, tiled=True)  13.9 us
    all_to_all x1, waiting for transfers between devices, on_device(): lax.all_to_all(copies, 'col', split_axis=0, concat_axis=0, tiled=True)  13.6 us
  transfers between devices with their start and end apart: 6, of which 6 were waited for; matrix products, arithmetic and copies ran while one was open for 9% of the time, Pallas kernels for 0%

commit v1 on v0

--- a/solution.py
+++ b/solution.py
@@ -79,9 +79,9 @@
         rho = jnp.take(band_v, val_index, axis=0) * jnp.take(band_c, cond_index, axis=0)
         z_all = jnp.einsum("phxyz,hzcjt->hcpxyjt", rho, table_z, precision=HIGH)
         z_all = z_all.reshape((mesh_cols,) + z_all.shape[2:])
-        if i >= 2:
-            z_all, pieces[i - 2] = lax.optimization_barrier((z_all, pieces[i - 2]))
         z_mine = lax.all_to_all(z_all, "col", split_axis=0, concat_axis=0, tiled=True)
+        if i >= 1:
+            z_mine, pieces[i - 1] = lax.optimization_barrier((z_mine, pieces[i - 1]))
         y_all = jnp.einsum("spxyjt,syteu->ejuxp", z_mine, table_y, precision=HIGH)
         flat = y_all.reshape(GRID * span_z, 2, chunk, pairs)
         chosen = jnp.take(flat, pick, axis=0)

time: 371 us -> 352 us (0.949)
  waiting for transfers between devices: 185 us -> 161 us
  other arithmetic: 38.2 us -> 42.5 us
    all_to_all x2, waiting for transfers between devices: 103 us -> 79.3 us  [on_device(): lax.all_to_all(z_all, 'col', split_axis=0, concat_axis=0, tiled=True)]
    select_n x1 -> x2, other arithmetic: 6.03 us -> 11.3 us  [on_device(): chosen = jnp.take(flat, pick, axis=0)]
  transfers between devices with their start and end apart: 6 -> 6, of which waited for: 6 -> 6; matrix products, arithmetic and copies ran while one was open for 9% -> 17% of each run, Pallas kernels for 0% -> 0%
where the time goes in v1:
time: 352 us; the launch traced here: 348 us
  waiting for transfers between devices  161 us (46%)
  local copies, waits for them, and re-layouts  67.9 us (19%)
  matrix products  46.9 us (13%)
  other arithmetic  42.5 us (12%)
  starting transfers between devices  29.5 us (8%)
    all_to_all x2, waiting for transfers between devices, on_device(): lax.all_to_all(z_all, 'col', split_axis=0, concat_axis=0, tiled=True)  79.3 us
    ppermute x1, waiting for transfers between devices, on_device(): cols = lax.ppermute(send, ('row', 'col'), perm)  45.2 us
    gather x2, local copies, waits for them, and re-layouts, on_device(): chosen = jnp.take(flat, pick, axis=0)  23.7 us
    dot_general x2, matrix products, on_device(): z_all = jnp.einsum('phxyz,hzcjt->hcpxyjt', rho, table_z, precision=HIGH)  20.4 us
    dot_general x2, matrix products, on_device(): y_all = jnp.einsum('spxyjt,syteu->ejuxp', z_mine, table_y, precision=HIGH)  19 us
    all_to_all x1, waiting for transfers between devices, on_device(): lax.all_to_all(spread, 'row', split_axis=0, concat_axis=0, tiled=True)  16 us
    all_to_all x2, starting transfers between devices, on_device(): lax.all_to_all(z_all, 'col', split_axis=0, concat_axis=0, tiled=True)  13.9 us
    all_to_all x1, waiting for transfers between devices, on_device(): lax.all_to_all(copies, 'col', split_axis=0, concat_axis=0, tiled=True)  13.6 us
  transfers between devices with their start and end apart: 6, of which 6 were waited for; matrix products, arithmetic and copies ran while one was open for 17% of the time, Pallas kernels for 0%

profile of v1, /device:TPU:24, one launch (start us, length us, event | category | flops | bytes accessed | tf_op | source)
XLA Modules:
  0.0 348.3 jit_solution(7653037168213127151)
XLA Ops:
  0.0 0.7 compare_select_fusion.4
  0.7 0.7 compare_and_fusion.1
  2.1 2.6 slice_bitcast_fusion.7
  4.8 1.8 pad_maximum_fusion.1
  6.5 4.4 %gather_fusion = f32[128,2,4,8,128]{4,3,2,1,0:T(8,128)} fusion(f32[64,2,4,8,128]{4,3,2,0,1:T(8,128)} %get-tuple-element.54, s32[1024]{0:T(1024)S(1)} %pad_clamp_fusion.1), kind=kCustom, calls=%fused_computation.clone | custom fusion | bytes 8389120 | tf_op jit(solution)/shard_map/jit(_take)/gather | solution.py:79
  10.9 2.8 gather_fusion.2
  13.7 2.6 slice_bitcast_fusion.5
  16.3 1.8 pad_maximum_fusion.2
  18.1 4.4 %gather_fusion.1 = f32[128,2,4,8,128]{4,3,2,1,0:T(8,128)} fusion(f32[64,2,4,8,128]{4,3,2,0,1:T(8,128)} %get-tuple-element.48, s32[1024]{0:T(1024)S(1)} %pad_clamp_fusion), kind=kCustom, calls=%fused_computation.2.clone | custom fusion | bytes 8389120 | tf_op jit(solution)/shard_map/jit(_take)/gather | solution.py:79
  22.5 2.8 gather_fusion.3
  25.3 8.8 %fusion.10 = (f32[128,2,4,8,128,1,1]{4,3,2,1,0,6,5:T(8,128)S(1)}, f32[128,2,4,8,128,1,1]{4,3,2,1,0,6,5:T(8,128)}) fusion(f32[128,2,4,8,128]{4,3,2,1,0:T(8,128)} %gather_fusion.3, f32[128,2,4,8,128]{4,3,2,1,0:T(8,128)} %gather_fusion.2, pred[128]{0:T(512)(128)(4,1)S(1)} %get-tuple-element.52, pred[128]{0:T(512)(128)(4,1)S(1)} %get-tuple-element.53, ...), kind=kLoop, calls=%fused_computation.18 | loop fusion | flops 6291456 | bytes 25166080 | tf_op jit(solution)/shard_map/mul | solution.py:79
  34.1 9.0 %fusion.6 = f32[2,8,9,2,128,4,8]{4,2,6,5,3,1,0:T(8,128)S(1)} fusion(f32[128,2,4,8,128,1,1]{4,3,2,1,0,6,5:T(8,128)S(1)} %get-tuple-element.46, f32[1,128,8,9,2]{1,3,4,2,0:T(8,128)S(1)} %reverse_bitcast_fusion, f32[1,128,8,9,1]{1,3,4,2,0:T(8,128)S(1)} %get-tuple-element.43, f32[1,128,8,9,1]{1,3,4,2,0:T(8,128)S(1)} %get-tuple-element.42), kind=kOutput, calls=%fused_computation.13 | convolution fusion | flops 1812013056 | bytes 9060352 | tf_op jit(solution)/shard_map/phxyz,hzcjt->hcpxyjt/dot_general | solution.py:80
  43.1 4.4 %copy.72 = f32[16,128,4,8,9,2]{1,3,5,4,2,0:T(8,128)} copy(f32[16,128,4,8,9,2]{1,4,3,2,5,0:T(8,128)S(1)} %bitcast.144) | data formatting | bytes 9437184 | tf_op jit(solution)/shard_map/reshape | solution.py:81
  47.5 7.2 %all-to-all-start.1 = ((f32[16,128,4,8,9,2]{1,3,5,4,2,0:T(8,128)}), f32[16,128,4,8,9,2]{1,3,5,4,2,0:T(8,128)}, u32[]{:S(2)}, u32[]{:S(2)}) async-start(f32[16,128,4,8,9,2]{1,3,5,4,2,0:T(8,128)} %copy.72), calls=%async_computation.1 | async-start | bytes 9437184 | tf_op jit(solution)/shard_map/all_to_all | solution.py:82
  54.7 11.4 %fusion.8 = f32[2,8,9,2,128,4,8]{4,2,6,5,3,1,0:T(8,128)S(1)} fusion(f32[128,2,4,8,128,1,1]{4,3,2,1,0,6,5:T(8,128)} %get-tuple-element.47, f32[1,128,8,9,2]{1,3,4,2,0:T(8,128)S(1)} %reverse_bitcast_fusion, f32[1,128,8,9,1]{1,3,4,2,0:T(8,128)S(1)} %get-tuple-element.43, f32[1,128,8,9,1]{1,3,4,2,0:T(8,128)S(1)} %get-tuple-element.42), kind=kOutput, calls=%fused_computation.15 | convolution fusion | flops 1812013056 | bytes 9060352 | tf_op jit(solution)/shard_map/phxyz,hzcjt->hcpxyjt/dot_general | solution.py:80
  66.1 4.3 %copy.70 = f32[16,128,4,8,9,2]{1,3,5,4,2,0:T(8,128)} copy(f32[16,128,4,8,9,2]{1,4,3,2,5,0:T(8,128)S(1)} %bitcast.143) | data formatting | bytes 9437184 | tf_op jit(solution)/shard_map/reshape | solution.py:81
  70.4 53.9 %all-to-all-done.1 = f32[16,128,4,8,9,2]{1,3,5,4,2,0:T(8,128)} async-done(((f32[16,128,4,8,9,2]{1,3,5,4,2,0:T(8,128)}), f32[16,128,4,8,9,2]{1,3,5,4,2,0:T(8,128)}, u32[]{:S(2)}, u32[]{:S(2)}) %all-to-all-start.1) | async-done | bytes 4718624 | tf_op jit(solution)/shard_map/all_to_all | solution.py:82
  124.3 6.7 %all-to-all-start = ((f32[16,128,4,8,9,2]{1,3,5,4,2,0:T(8,128)}), f32[16,128,4,8,9,2]{1,3,5,4,2,0:T(8,128)}, u32[]{:S(2)}, u32[]{:S(2)}) async-start(f32[16,128,4,8,9,2]{1,3,5,4,2,0:T(8,128)} %copy.70), calls=%async_computation | async-start | bytes 9437184 | tf_op jit(solution)/shard_map/all_to_all | solution.py:82
  131.7 2.1 fusion.28
  134.2 9.5 %fusion.12 = f32[128,9,2,4,128]{4,0,1,3,2:T(8,128)S(1)} fusion(f32[16,128,4,8,9,2]{1,3,5,4,2,0:T(8,128)} %all-to-all-done.1, f32[16,8,1,128,1]{3,0,1,2,4:T(8,128)S(1)} %get-tuple-element.41, f32[16,8,1,128,1]{3,0,1,2,4:T(8,128)S(1)} %get-tuple-element.40, f32[16,8,1,128,1]{3,0,1,2,4:T(8,128)S(1)} %get-tuple-element.39), kind=kOutput, calls=%fused_computation.21 | convolution fusion | flops 3624075264 | bytes 9633792 | tf_op jit(solution)/shard_map/spxyjt,syteu->ejuxp/dot_general | solution.py:85
  143.7 5.3 %copy.74 = f32[128,9,2,4,128]{4,3,2,1,0:T(4,128)} copy(f32[128,9,2,4,128]{4,0,1,3,2:T(8,128)S(1)} %fusion.12) | data formatting | bytes 9437184 | tf_op jit(solution)/shard_map/spxyjt,syteu->ejuxp/transpose | solution.py:85
  149.0 11.8 %gather_fusion.4 = f32[1024,2,4,128]{3,2,1,0:T(4,128)} fusion(f32[1152,2,4,128]{3,2,1,0:T(4,128)} %bitcast.146, s32[1024]{0:T(1024)S(1)} %broadcast_clamp_fusion), kind=kCustom, calls=%fused_computation.1.clone | custom fusion | bytes 8392704 | tf_op jit(solution)/shard_map/jit(_take)/gather | solution.py:87
  160.8 5.7 %broadcast_select_fusion.1 = f32[1024,2,4,128]{3,2,1,0:T(4,128)S(1)} fusion(f32[1024,2,4,128]{3,2,1,0:T(4,128)} %gather_fusion.4, pred[1024]{0:T(1024)(128)(4,1)S(1)} %get-tuple-element.15), kind=kLoop, calls=%fused_computation.38 | loop fusion | flops 1048576 | bytes 8389632 | tf_op jit(solution)/shard_map/jit(_take)/select_n | solution.py:87
  166.5 6.5 %add_reduce_fusion.1 = (f32[1024,128]{1,0:T(8,128)S(1)}, f32[1024,128]{1,0:T(8,128)S(1)}) fusion(f32[1024,2,4,128]{3,2,1,0:T(4,128)S(1)} %broadcast_select_fusion.1, f32[1024,4]{1,0:T(8,128)S(1)} %get-tuple-element.34, f32[1024,4]{1,0:T(8,128)S(1)} %get-tuple-element.56), kind=kLoop, calls=%fused_computation.42 | loop fusion | flops 3932160 | bytes 5275648 | tf_op jit(solution)/shard_map/reduce_sum | solution.py:92
  173.1 25.4 %all-to-all-done = f32[16,128,4,8,9,2]{1,3,5,4,2,0:T(8,128)} async-done(((f32[16,128,4,8,9,2]{1,3,5,4,2,0:T(8,128)}), f32[16,128,4,8,9,2]{1,3,5,4,2,0:T(8,128)}, u32[]{:S(2)}, u32[]{:S(2)}) %all-to-all-start) | async-done | bytes 4718624 | tf_op jit(solution)/shard_map/all_to_all | solution.py:82
  198.4 9.5 %fusion.15 = f32[128,9,2,4,128]{4,0,1,3,2:T(8,128)S(1)} fusion(f32[16,128,4,8,9,2]{1,3,5,4,2,0:T(8,128)} %all-to-all-done, f32[16,8,1,128,1]{3,0,1,2,4:T(8,128)S(1)} %get-tuple-element.41, f32[16,8,1,128,1]{3,0,1,2,4:T(8,128)S(1)} %get-tuple-element.40, f32[16,8,1,128,1]{3,0,1,2,4:T(8,128)S(1)} %get-tuple-element.39), kind=kOutput, calls=%fused_computation.22 | convolution fusion | flops 3624075264 | bytes 9633792 | tf_op jit(solution)/shard_map/spxyjt,syteu->ejuxp/dot_general | solution.py:85
  207.9 5.2 %copy.77 = f32[128,9,2,4,128]{4,3,2,1,0:T(4,128)} copy(f32[128,9,2,4,128]{4,0,1,3,2:T(8,128)S(1)} %fusion.15) | data formatting | bytes 9437184 | tf_op jit(solution)/shard_map/spxyjt,syteu->ejuxp/transpose | solution.py:85
  213.1 11.8 %gather_fusion.5 = f32[1024,2,4,128]{3,2,1,0:T(4,128)} fusion(f32[1152,2,4,128]{3,2,1,0:T(4,128)} %bitcast.145, s32[1024]{0:T(1024)S(1)} %broadcast_clamp_fusion), kind=kCustom, calls=%fused_computation.5.clone | custom fusion | bytes 8392704 | tf_op jit(solution)/shard_map/jit(_take)/gather | solution.py:87
  224.9 5.7 %broadcast_select_fusion = f32[1024,2,4,128]{3,2,1,0:T(4,128)S(1)} fusion(f32[1024,2,4,128]{3,2,1,0:T(4,128)} %gather_fusion.5, pred[1024]{0:T(1024)(128)(4,1)S(1)} %get-tuple-element.15), kind=kLoop, calls=%fused_computation.37 | loop fusion | flops 1048576 | bytes 8389632 | tf_op jit(solution)/shard_map/jit(_take)/select_n | solution.py:87
  230.6 6.3 %add_reduce_fusion = (f32[1024,128]{1,0:T(8,128)S(1)}, f32[1024,128]{1,0:T(8,128)S(1)}) fusion(f32[1024,2,4,128]{3,2,1,0:T(4,128)S(1)} %broadcast_select_fusion, f32[1024,4]{1,0:T(8,128)S(1)} %get-tuple-element.33, f32[1024,4]{1,0:T(8,128)S(1)} %get-tuple-element.57), kind=kLoop, calls=%fused_computation.40 | loop fusion | flops 3932160 | bytes 5275648 | tf_op jit(solution)/shard_map/reduce_sum | solution.py:92
  236.9 0.4 fusion.23
  237.3 1.1 copy.79
  238.4 5.5 %all-to-all-start.2 = ((f32[8,128,2,128]{3,1,2,0:T(8,128)}), f32[8,128,2,128]{3,1,2,0:T(8,128)S(1)}, u32[]{:S(2)}, u32[]{:S(2)}) async-start(f32[8,128,2,128]{3,1,2,0:T(8,128)} %copy.79), calls=%async_computation.2 | async-start | bytes 2097152 | tf_op jit(solution)/shard_map/all_to_all | solution.py:101
  243.9 16.0 %all-to-all-done.2 = f32[8,128,2,128]{3,1,2,0:T(8,128)S(1)} async-done(((f32[8,128,2,128]{3,1,2,0:T(8,128)}), f32[8,128,2,128]{3,1,2,0:T(8,128)S(1)}, u32[]{:S(2)}, u32[]{:S(2)}) %all-to-all-start.2) | async-done | bytes 1048608 | tf_op jit(solution)/shard_map/all_to_all | solution.py:101
  259.9 0.9 collective-permute-start
  260.8 6.8 %collective-permute-done = f32[64,2,128]{2,0,1:T(8,128)S(1)} collective-permute-done((f32[64,2,128]{2,0,1:T(8,128)S(1)}, f32[64,2,128]{2,0,1:T(8,128)S(1)}, u32[]{:S(2)}, u32[]{:S(2)}) %collective-permute-start) | collective-permute-done | bytes 65568 | tf_op jit(solution)/shard_map/ppermute | solution.py:105
  267.7 1.4 broadcast_in_dim.74
  269.1 4.5 %all-to-all-start.3 = ((f32[16,64,2,128]{3,2,1,0:T(2,128)}), f32[16,64,2,128]{3,2,1,0:T(2,128)S(1)}, u32[]{:S(2)}, u32[]{:S(2)}) async-start(f32[16,64,2,128]{3,2,1,0:T(2,128)} %broadcast_in_dim.74), calls=%async_computation.3 | async-start | bytes 2097152 | tf_op jit(solution)/shard_map/all_to_all | solution.py:108
  273.6 13.6 %all-to-all-done.3 = f32[16,64,2,128]{3,2,1,0:T(2,128)S(1)} async-done(((f32[16,64,2,128]{3,2,1,0:T(2,128)}), f32[16,64,2,128]{3,2,1,0:T(2,128)S(1)}, u32[]{:S(2)}, u32[]{:S(2)}) %all-to-all-start.3) | async-done | bytes 1048608 | tf_op jit(solution)/shard_map/all_to_all | solution.py:108
  287.2 4.7 %collective-permute-start.1 = (f32[512,2,128]{2,1,0:T(2,128)S(1)}, f32[512,2,128]{2,1,0:T(2,128)S(1)}, u32[]{:S(2)}, u32[]{:S(2)}) collective-permute-start(f32[512,2,128]{2,1,0:T(2,128)S(1)} %constant_dynamic-slice_fusion), channel_id=1, source_target_pairs={{0,0},{1,16},{2,32},{3,48},{4,64},{5,80},{6,96},{7,112},{8,1},{9,1... | collective-permute-start | bytes 1572872 | tf_op jit(solution)/shard_map/ppermute | solution.py:118
  292.1 0.7 slice_multiply_fusion
  292.8 45.2 %collective-permute-done.1 = f32[512,2,128]{2,1,0:T(2,128)S(1)} collective-permute-done((f32[512,2,128]{2,1,0:T(2,128)S(1)}, f32[512,2,128]{2,1,0:T(2,128)S(1)}, u32[]{:S(2)}, u32[]{:S(2)}) %collective-permute-start.1) | collective-permute-done | bytes 524320 | tf_op jit(solution)/shard_map/ppermute | solution.py:118
  338.1 0.4 fusion.77
  338.5 1.8 fusion.79
  340.3 1.8 fusion.78
  342.1 1.8 fusion.80
  343.9 2.1 fusion.21
  346.1 2.0 copy-done.7
  (45 shorter events, 2.1 us)
Async XLA Ops:
  47.5 76.8 %all-to-all-start.1 = ((f32[16,128,4,8,9,2]{1,3,5,4,2,0:T(8,128)}), f32[16,128,4,8,9,2]{1,3,5,4,2,0:T(8,128)}, u32[]{:S(2)}, u32[]{:S(2)}) async-start(f32[16,128,4,8,9,2]{1,3,5,4,2,0:T(8,128)} %copy.72), calls=%async_computation.1 | async-start | bytes 9437184 | tf_op jit(solution)/shard_map/all_to_all | solution.py:82
  70.4 60.7 %copy-start.1 = (s32[8192]{0:T(1024)S(1)}, s32[8192]{0:T(1024)}, u32[]{:S(2)}) copy-start(s32[8192]{0:T(1024)} %param.18) | copy-start | bytes 98308
  124.3 74.1 %all-to-all-start = ((f32[16,128,4,8,9,2]{1,3,5,4,2,0:T(8,128)}), f32[16,128,4,8,9,2]{1,3,5,4,2,0:T(8,128)}, u32[]{:S(2)}, u32[]{:S(2)}) async-start(f32[16,128,4,8,9,2]{1,3,5,4,2,0:T(8,128)} %copy.70), calls=%async_computation | async-start | bytes 9437184 | tf_op jit(solution)/shard_map/all_to_all | solution.py:82
  238.4 53.5 %copy-start.2 = (s32[128]{0:T(128)S(1)}, s32[128]{0:T(128)}, u32[]{:S(2)}) copy-start(s32[128]{0:T(128)} %param.17) | copy-start | bytes 1540
  238.4 53.6 %copy-start.3 = (s32[128]{0:T(128)S(1)}, s32[128]{0:T(128)}, u32[]{:S(2)}) copy-start(s32[128]{0:T(128)} %param.16) | copy-start | bytes 1540
  238.4 53.6 %copy-start.4 = (f32[64]{0:T(128)S(1)}, f32[64]{0:T(128)}, u32[]{:S(2)}) copy-start(f32[64]{0:T(128)} %param.14) | copy-start | bytes 772
  238.4 53.6 %copy-start.5 = (f32[64]{0:T(128)S(1)}, f32[64]{0:T(128)}, u32[]{:S(2)}) copy-start(f32[64]{0:T(128)} %param.15) | copy-start | bytes 772
  238.4 21.5 %all-to-all-start.2 = ((f32[8,128,2,128]{3,1,2,0:T(8,128)}), f32[8,128,2,128]{3,1,2,0:T(8,128)S(1)}, u32[]{:S(2)}, u32[]{:S(2)}) async-start(f32[8,128,2,128]{3,1,2,0:T(8,128)} %copy.79), calls=%async_computation.2 | async-start | bytes 2097152 | tf_op jit(solution)/shard_map/all_to_all | solution.py:101
  259.9 7.7 %collective-permute-start = (f32[64,2,128]{2,0,1:T(8,128)S(1)}, f32[64,2,128]{2,0,1:T(8,128)S(1)}, u32[]{:S(2)}, u32[]{:S(2)}) collective-permute-start(f32[64,2,128]{2,0,1:T(8,128)S(1)} %dynamic-slice_bitcast_fusion), channel_id=1, source_target_pairs={{0,15},{1,14},{2,13},{3,12},{4,11},{5,10},{6,9},{7,8},{8,7},{9,6},... | collective-permute-start | bytes 196616 | tf_op jit(solution)/shard_map/ppermute | solution.py:105
  269.1 18.1 %all-to-all-start.3 = ((f32[16,64,2,128]{3,2,1,0:T(2,128)}), f32[16,64,2,128]{3,2,1,0:T(2,128)S(1)}, u32[]{:S(2)}, u32[]{:S(2)}) async-start(f32[16,64,2,128]{3,2,1,0:T(2,128)} %broadcast_in_dim.74), calls=%async_computation.3 | async-start | bytes 2097152 | tf_op jit(solution)/shard_map/all_to_all | solution.py:108
  287.2 50.8 %collective-permute-start.1 = (f32[512,2,128]{2,1,0:T(2,128)S(1)}, f32[512,2,128]{2,1,0:T(2,128)S(1)}, u32[]{:S(2)}, u32[]{:S(2)}) collective-permute-start(f32[512,2,128]{2,1,0:T(2,128)S(1)} %constant_dynamic-slice_fusion), channel_id=1, source_target_pairs={{0,0},{1,16},{2,32},{3,48},{4,64},{5,80},{6,96},{7,112},{8,1},{9,1... | collective-permute-start | bytes 1572872 | tf_op jit(solution)/shard_map/ppermute | solution.py:118
  338.5 5.4 %copy-start = (f32[2,1024,512]{2,1,0:T(8,128)S(1)}, f32[2,1024,512]{2,1,0:T(8,128)}, u32[]{:S(2)}) copy-start(f32[2,1024,512]{2,1,0:T(8,128)} %param.19) | copy-start | bytes 12582916
  338.5 5.4 %copy-start.6 = (f32[2,1024,512]{2,1,0:T(8,128)S(1)}, f32[2,1024,512]{2,1,0:T(8,128)}, u32[]{:S(2)}) copy-start(f32[2,1024,512]{2,1,0:T(8,128)} %custom-call.12) | copy-start | bytes 12582916
  346.0 2.0 copy-start.7

commit v2 on v1

--- a/solution.py
+++ b/solution.py
@@ -98,15 +98,20 @@
     partial = partial * jnp.stack([jnp.ones_like(sign), sign], axis=1)[:, :, None] * scale
     block = 2 * per_device
     spread = partial.reshape(mesh_rows, block, 2, pairs)
-    gathered = lax.all_to_all(spread, "row", split_axis=0, concat_axis=0, tiled=True)
-    both_blocks = jnp.sum(gathered, axis=0).reshape(2, per_device, 2, pairs)
+    summed = lax.dynamic_index_in_dim(spread, row_pos, axis=0, keepdims=False)
+    for k in range(1, mesh_rows):
+        out = lax.dynamic_index_in_dim(spread, (row_pos + k) % mesh_rows, axis=0, keepdims=False)
+        summed = summed + lax.ppermute(out, "row", [(r, (r + k) % mesh_rows) for r in range(mesh_rows)])
+    both_blocks = summed.reshape(2, per_device, 2, pairs)
     mine = lax.dynamic_index_in_dim(both_blocks, side, axis=0, keepdims=False)
     theirs = lax.dynamic_index_in_dim(both_blocks, 1 - side, axis=0, keepdims=False)
     partner = lax.ppermute(theirs, "col", [(c, mesh_cols - 1 - c) for c in range(mesh_cols)])
     own = mine + partner
-    copies = jnp.broadcast_to(own[None], (mesh_cols,) + own.shape)
-    row_blocks = lax.all_to_all(copies, "col", split_axis=0, concat_axis=0, tiled=True)
-    rows = row_blocks.reshape(mesh_cols * per_device, 2, pairs)
+    arrived = [own]
+    for k in range(1, mesh_cols):
+        arrived.append(lax.ppermute(own, "col", [(c, (c + k) % mesh_cols) for c in range(mesh_cols)]))
+    order = (col_pos - jnp.arange(mesh_cols, dtype=jnp.int32)) % mesh_cols
+    rows = jnp.take(jnp.stack(arrived), order, axis=0).reshape(mesh_cols * per_device, 2, pairs)
     half = mesh_cols // 2
     send = lax.dynamic_slice_in_dim(rows, (col_pos // half) * half * per_device, half * per_device, 0)
     perm = []

time: 352 us -> 365 us (1.037)
  starting transfers between devices: 29.5 us -> 49.8 us
  waiting for transfers between devices: 161 us -> 152 us
  other arithmetic: 42.5 us -> 46.8 us
  local copies, waits for them, and re-layouts: 67.9 us -> 64.2 us
    ppermute x0 -> x22, starting transfers between devices: none -> 30.7 us  [the longest x15 23 us: on_device(): lax.ppermute(own, 'col', [(c, (c + k) % mesh_cols) for c in range(mesh_co...]
    all_to_all x2 -> x0, waiting for transfers between devices: 29.6 us -> none  [the longest x1 16 us: on_device(): lax.all_to_all(spread, 'row', split_axis=0, concat_axis=0, tiled=True)]
    ppermute x0 -> x22, waiting for transfers between devices: none -> 18.9 us  [the longest x7 12.2 us: on_device(): lax.ppermute(out, 'row', [(r, (r + k) % mesh_rows) for r in range(mesh_ro...]
    all_to_all x2 -> x0, starting transfers between devices: 10 us -> none  [the longest x1 5.49 us: on_device(): lax.all_to_all(spread, 'row', split_axis=0, concat_axis=0, tiled=True)]
  transfers between devices with their start and end apart: 6 -> 26, of which waited for: 6 -> 14; matrix products, arithmetic and copies ran while one was open for 17% -> 16% of each run, Pallas kernels for 0% -> 0%
where the time goes in v2:
time: 365 us; the launch traced here: 361 us
  waiting for transfers between devices  152 us (42%)
  local copies, waits for them, and re-layouts  64.2 us (18%)
  starting transfers between devices  49.8 us (14%)
  matrix products  47 us (13%)
  other arithmetic  46.8 us (13%)
    all_to_all x2, waiting for transfers between devices, on_device(): lax.all_to_all(z_all, 'col', split_axis=0, concat_axis=0, tiled=True)  79.2 us
    ppermute x1, waiting for transfers between devices, on_device(): cols = lax.ppermute(send, ('row', 'col'), perm)  46.4 us
    gather x2, local copies, waits for them, and re-layouts, on_device(): chosen = jnp.take(flat, pick, axis=0)  23.7 us
    ppermute x15, starting transfers between devices, on_device(): lax.ppermute(own, 'col', [(c, (c + k) % mesh_cols) for c in range(mesh_co...  23 us
    dot_general x2, matrix products, on_device(): z_all = jnp.einsum('phxyz,hzcjt->hcpxyjt', rho, table_z, precision=HIGH)  20.4 us
    dot_general x2, matrix products, on_device(): y_all = jnp.einsum('spxyjt,syteu->ejuxp', z_mine, table_y, precision=HIGH)  19 us
    all_to_all x2, starting transfers between devices, on_device(): lax.all_to_all(z_all, 'col', split_axis=0, concat_axis=0, tiled=True)  13.9 us
    reduce_sum x2, other arithmetic, on_device(): part_re = jnp.sum(c_re * cx + c_im * sx, axis=1)  12.8 us
  transfers between devices with their start and end apart: 26, of which 14 were waited for; matrix products, arithmetic and copies ran while one was open for 16% of the time, Pallas kernels for 0%

profile of v2, /device:TPU:24, one launch (start us, length us, event | category | flops | bytes accessed | tf_op | source)
XLA Modules:
  0.0 361.1 jit_solution(11694440871970179909)
XLA Ops:
  2.1 2.8 slice_bitcast_fusion.5
  5.6 1.8 slice_bitcast_fusion.7
  7.4 2.0 pad_maximum_fusion.2
  9.4 4.4 %gather_fusion.4 = f32[128,2,4,8,128]{4,3,2,1,0:T(8,128)} fusion(f32[64,2,4,8,128]{4,3,2,0,1:T(8,128)} %get-tuple-element.52, s32[1024]{0:T(1024)S(1)} %pad_clamp_fusion.1), kind=kCustom, calls=%fused_computation.4.clone | custom fusion | bytes 8389120 | tf_op jit(solution)/shard_map/jit(_take)/gather | solution.py:79
  13.8 2.8 gather_fusion.2
  16.6 3.9 %pad_maximum_fusion.1 = (f32[64,2,4,8,128]{4,3,2,0,1:T(8,128)S(1)}, f32[64,2,4,8,128]{4,3,2,0,1:T(8,128)}) fusion(f32[64,1,4,8,128]{4,3,2,0,1:T(8,128)} %get-tuple-element.20, f32[64,1,4,8,128]{4,3,2,0,1:T(8,128)} %get-tuple-element.21, f32[64,1,4,8,128]{4,3,2,0,1:T(8,128)} %get-tuple-element.22, f32[64,1,4,8,128]{4,3,2,0,1:T(8,128)S(1)} %get-tuple-element.19), kind=kLoop, calls=%fused_computation.28 | loop fusion | flops 1048576 | bytes 8388608 | tf_op jit(solution)/shard_map/stack | solution.py:77
  20.5 4.4 %gather_fusion.3 = f32[128,2,4,8,128]{4,3,2,1,0:T(8,128)} fusion(f32[64,2,4,8,128]{4,3,2,0,1:T(8,128)} %get-tuple-element.58, s32[1024]{0:T(1024)S(1)} %pad_clamp_fusion.2), kind=kCustom, calls=%fused_computation.3.clone | custom fusion | bytes 8389120 | tf_op jit(solution)/shard_map/jit(_take)/gather | solution.py:79
  24.9 2.8 gather_fusion.1
  27.7 8.8 %fusion.10 = (f32[128,2,4,8,128,1,1]{4,3,2,1,0,6,5:T(8,128)S(1)}, f32[128,2,4,8,128,1,1]{4,3,2,1,0,6,5:T(8,128)}) fusion(f32[128,2,4,8,128]{4,3,2,1,0:T(8,128)} %gather_fusion.4, f32[128,2,4,8,128]{4,3,2,1,0:T(8,128)} %gather_fusion.3, pred[128]{0:T(512)(128)(4,1)S(1)} %get-tuple-element.55, pred[128]{0:T(512)(128)(4,1)S(1)} %get-tuple-element.56, ...), kind=kLoop, calls=%fused_computation.19 | loop fusion | flops 6291456 | bytes 25166080 | tf_op jit(solution)/shard_map/mul | solution.py:79
  36.5 9.0 %fusion.6 = f32[2,8,9,2,128,4,8]{4,2,6,5,3,1,0:T(8,128)S(1)} fusion(f32[128,2,4,8,128,1,1]{4,3,2,1,0,6,5:T(8,128)S(1)} %get-tuple-element.49, f32[1,128,8,9,2]{1,3,4,2,0:T(8,128)S(1)} %reverse_bitcast_fusion, f32[1,128,8,9,1]{1,3,4,2,0:T(8,128)S(1)} %get-tuple-element.46, f32[1,128,8,9,1]{1,3,4,2,0:T(8,128)S(1)} %get-tuple-element.45), kind=kOutput, calls=%fused_computation.14 | convolution fusion | flops 1812013056 | bytes 9060352 | tf_op jit(solution)/shard_map/phxyz,hzcjt->hcpxyjt/dot_general | solution.py:80
  45.5 4.4 %copy.55 = f32[16,128,4,8,9,2]{1,3,5,4,2,0:T(8,128)} copy(f32[16,128,4,8,9,2]{1,4,3,2,5,0:T(8,128)S(1)} %bitcast.212) | data formatting | bytes 9437184 | tf_op jit(solution)/shard_map/reshape | solution.py:81
  49.9 7.2 %all-to-all-start.1 = ((f32[16,128,4,8,9,2]{1,3,5,4,2,0:T(8,128)}), f32[16,128,4,8,9,2]{1,3,5,4,2,0:T(8,128)}, u32[]{:S(2)}, u32[]{:S(2)}) async-start(f32[16,128,4,8,9,2]{1,3,5,4,2,0:T(8,128)} %copy.55), calls=%async_computation.1 | async-start | bytes 9437184 | tf_op jit(solution)/shard_map/all_to_all | solution.py:82
  57.1 11.4 %fusion.8 = f32[2,8,9,2,128,4,8]{4,2,6,5,3,1,0:T(8,128)S(1)} fusion(f32[128,2,4,8,128,1,1]{4,3,2,1,0,6,5:T(8,128)} %get-tuple-element.50, f32[1,128,8,9,2]{1,3,4,2,0:T(8,128)S(1)} %reverse_bitcast_fusion, f32[1,128,8,9,1]{1,3,4,2,0:T(8,128)S(1)} %get-tuple-element.46, f32[1,128,8,9,1]{1,3,4,2,0:T(8,128)S(1)} %get-tuple-element.45), kind=kOutput, calls=%fused_computation.16 | convolution fusion | flops 1812013056 | bytes 9060352 | tf_op jit(solution)/shard_map/phxyz,hzcjt->hcpxyjt/dot_general | solution.py:80
  68.5 4.3 %copy.53 = f32[16,128,4,8,9,2]{1,3,5,4,2,0:T(8,128)} copy(f32[16,128,4,8,9,2]{1,4,3,2,5,0:T(8,128)S(1)} %bitcast.211) | data formatting | bytes 9437184 | tf_op jit(solution)/shard_map/reshape | solution.py:81
  72.8 53.9 %all-to-all-done.1 = f32[16,128,4,8,9,2]{1,3,5,4,2,0:T(8,128)} async-done(((f32[16,128,4,8,9,2]{1,3,5,4,2,0:T(8,128)}), f32[16,128,4,8,9,2]{1,3,5,4,2,0:T(8,128)}, u32[]{:S(2)}, u32[]{:S(2)}) %all-to-all-start.1) | async-done | bytes 4718624 | tf_op jit(solution)/shard_map/all_to_all | solution.py:82
  126.7 6.7 %all-to-all-start = ((f32[16,128,4,8,9,2]{1,3,5,4,2,0:T(8,128)}), f32[16,128,4,8,9,2]{1,3,5,4,2,0:T(8,128)}, u32[]{:S(2)}, u32[]{:S(2)}) async-start(f32[16,128,4,8,9,2]{1,3,5,4,2,0:T(8,128)} %copy.53), calls=%async_computation | async-start | bytes 9437184 | tf_op jit(solution)/shard_map/all_to_all | solution.py:82
  134.3 2.1 fusion.42
  136.7 9.5 %fusion.12 = f32[128,9,2,4,128]{4,0,1,3,2:T(8,128)S(1)} fusion(f32[16,128,4,8,9,2]{1,3,5,4,2,0:T(8,128)} %all-to-all-done.1, f32[16,8,1,128,1]{3,0,1,2,4:T(8,128)S(1)} %get-tuple-element.44, f32[16,8,1,128,1]{3,0,1,2,4:T(8,128)S(1)} %get-tuple-element.43, f32[16,8,1,128,1]{3,0,1,2,4:T(8,128)S(1)} %get-tuple-element.42), kind=kOutput, calls=%fused_computation.22 | convolution fusion | flops 3624075264 | bytes 9633792 | tf_op jit(solution)/shard_map/spxyjt,syteu->ejuxp/dot_general | solution.py:85
  146.2 5.3 %copy.57 = f32[128,9,2,4,128]{4,3,2,1,0:T(4,128)} copy(f32[128,9,2,4,128]{4,0,1,3,2:T(8,128)S(1)} %fusion.12) | data formatting | bytes 9437184 | tf_op jit(solution)/shard_map/spxyjt,syteu->ejuxp/transpose | solution.py:85
  151.5 11.8 %gather_fusion.5 = f32[1024,2,4,128]{3,2,1,0:T(4,128)} fusion(f32[1152,2,4,128]{3,2,1,0:T(4,128)} %bitcast.214, s32[1024]{0:T(1024)S(1)} %broadcast_clamp_fusion), kind=kCustom, calls=%fused_computation.1.clone | custom fusion | bytes 8392704 | tf_op jit(solution)/shard_map/jit(_take)/gather | solution.py:87
  163.3 5.7 %broadcast_select_fusion.1 = f32[1024,2,4,128]{3,2,1,0:T(4,128)S(1)} fusion(f32[1024,2,4,128]{3,2,1,0:T(4,128)} %gather_fusion.5, pred[1024]{0:T(1024)(128)(4,1)S(1)} %get-tuple-element.17), kind=kLoop, calls=%fused_computation.39 | loop fusion | flops 1048576 | bytes 8389632 | tf_op jit(solution)/shard_map/jit(_take)/select_n | solution.py:87
  169.0 6.5 %add_reduce_fusion.1 = (f32[1024,128]{1,0:T(8,128)S(1)}, f32[1024,128]{1,0:T(8,128)S(1)}) fusion(f32[1024,2,4,128]{3,2,1,0:T(4,128)S(1)} %broadcast_select_fusion.1, f32[1024,4]{1,0:T(8,128)S(1)} %get-tuple-element.37, f32[1024,4]{1,0:T(8,128)S(1)} %get-tuple-element.59), kind=kLoop, calls=%fused_computation.43 | loop fusion | flops 3932160 | bytes 5275648 | tf_op jit(solution)/shard_map/reduce_sum | solution.py:92
  175.6 25.3 %all-to-all-done = f32[16,128,4,8,9,2]{1,3,5,4,2,0:T(8,128)} async-done(((f32[16,128,4,8,9,2]{1,3,5,4,2,0:T(8,128)}), f32[16,128,4,8,9,2]{1,3,5,4,2,0:T(8,128)}, u32[]{:S(2)}, u32[]{:S(2)}) %all-to-all-start) | async-done | bytes 4718624 | tf_op jit(solution)/shard_map/all_to_all | solution.py:82
  200.8 9.5 %fusion.15 = f32[128,9,2,4,128]{4,0,1,3,2:T(8,128)S(1)} fusion(f32[16,128,4,8,9,2]{1,3,5,4,2,0:T(8,128)} %all-to-all-done, f32[16,8,1,128,1]{3,0,1,2,4:T(8,128)S(1)} %get-tuple-element.44, f32[16,8,1,128,1]{3,0,1,2,4:T(8,128)S(1)} %get-tuple-element.43, f32[16,8,1,128,1]{3,0,1,2,4:T(8,128)S(1)} %get-tuple-element.42), kind=kOutput, calls=%fused_computation.23 | convolution fusion | flops 3624075264 | bytes 9633792 | tf_op jit(solution)/shard_map/spxyjt,syteu->ejuxp/dot_general | solution.py:85
  210.3 5.2 %copy.60 = f32[128,9,2,4,128]{4,3,2,1,0:T(4,128)} copy(f32[128,9,2,4,128]{4,0,1,3,2:T(8,128)S(1)} %fusion.15) | data formatting | bytes 9437184 | tf_op jit(solution)/shard_map/spxyjt,syteu->ejuxp/transpose | solution.py:85
  215.5 11.8 %gather_fusion.6 = f32[1024,2,4,128]{3,2,1,0:T(4,128)} fusion(f32[1152,2,4,128]{3,2,1,0:T(4,128)} %bitcast.213, s32[1024]{0:T(1024)S(1)} %broadcast_clamp_fusion), kind=kCustom, calls=%fused_computation.5.clone | custom fusion | bytes 8392704 | tf_op jit(solution)/shard_map/jit(_take)/gather | solution.py:87
  227.3 5.7 %broadcast_select_fusion = f32[1024,2,4,128]{3,2,1,0:T(4,128)S(1)} fusion(f32[1024,2,4,128]{3,2,1,0:T(4,128)} %gather_fusion.6, pred[1024]{0:T(1024)(128)(4,1)S(1)} %get-tuple-element.17), kind=kLoop, calls=%fused_computation.38 | loop fusion | flops 1048576 | bytes 8389632 | tf_op jit(solution)/shard_map/jit(_take)/select_n | solution.py:87
  233.0 6.3 %add_reduce_fusion = (f32[1024,128]{1,0:T(8,128)S(1)}, f32[1024,128]{1,0:T(8,128)S(1)}) fusion(f32[1024,2,4,128]{3,2,1,0:T(4,128)S(1)} %broadcast_select_fusion, f32[1024,4]{1,0:T(8,128)S(1)} %get-tuple-element.36, f32[1024,4]{1,0:T(8,128)S(1)} %get-tuple-element.60), kind=kLoop, calls=%fused_computation.41 | loop fusion | flops 3932160 | bytes 5275648 | tf_op jit(solution)/shard_map/reduce_sum | solution.py:92
  241.0 2.9 collective-permute-start.5
  244.0 3.5 collective-permute-start.3
  249.8 4.2 %collective-permute-done.3 = f32[128,2,128]{2,0,1:T(8,128)S(1)} collective-permute-done((f32[128,2,128]{2,0,1:T(8,128)S(1)}, f32[128,2,128]{2,0,1:T(8,128)S(1)}, u32[]{:S(2)}, u32[]{:S(2)}) %collective-permute-start.3) | collective-permute-done | bytes 131104 | tf_op jit(solution)/shard_map/ppermute | solution.py:104
  254.8 5.0 %collective-permute-done.1 = f32[128,2,128]{2,0,1:T(8,128)S(1)} collective-permute-done((f32[128,2,128]{2,0,1:T(8,128)S(1)}, f32[128,2,128]{2,0,1:T(8,128)S(1)}, u32[]{:S(2)}, u32[]{:S(2)}) %collective-permute-start.1) | collective-permute-done | bytes 131104 | tf_op jit(solution)/shard_map/ppermute | solution.py:104
  260.9 8.0 %collective-permute-done.7 = f32[64,2,128]{2,0,1:T(8,128)S(1)} collective-permute-done((f32[64,2,128]{2,0,1:T(8,128)S(1)}, f32[64,2,128]{2,0,1:T(8,128)S(1)}, u32[]{:S(2)}, u32[]{:S(2)}) %collective-permute-start.7) | collective-permute-done | bytes 65568 | tf_op jit(solution)/shard_map/ppermute | solution.py:108
  269.2 2.0 collective-permute-start.10
  271.1 2.0 collective-permute-start.12
  273.1 4.5 %collective-permute-done.8 = f32[64,2,128]{2,0,1:T(8,128)S(1)} collective-permute-done((f32[64,2,128]{2,0,1:T(8,128)S(1)}, f32[64,2,128]{2,0,1:T(8,128)S(1)}, u32[]{:S(2)}, u32[]{:S(2)}) %collective-permute-start.8) | collective-permute-done | bytes 65568 | tf_op jit(solution)/shard_map/ppermute | solution.py:112
  279.0 3.8 %collective-permute-start.15 = (f32[64,2,128]{2,0,1:T(8,128)S(1)}, f32[64,2,128]{2,0,1:T(8,128)S(1)}, u32[]{:S(2)}, u32[]{:S(2)}) collective-permute-start(f32[64,2,128]{2,0,1:T(8,128)S(1)} %get-tuple-element.16), channel_id=1, source_target_pairs={{0,8},{1,9},{2,10},{3,11},{4,12},{5,13},{6,14},{7,15},{8,0},{9,1},... | collective-permute-start | bytes 196616 | tf_op jit(solution)/shard_map/ppermute | solution.py:112
  282.9 5.4 %collective-permute-start.17 = (f32[64,2,128]{2,0,1:T(8,128)S(1)}, f32[64,2,128]{2,0,1:T(8,128)S(1)}, u32[]{:S(2)}, u32[]{:S(2)}) collective-permute-start(f32[64,2,128]{2,0,1:T(8,128)S(1)} %get-tuple-element.16), channel_id=1, source_target_pairs={{0,10},{1,11},{2,12},{3,13},{4,14},{5,15},{6,0},{7,1},{8,2},{9,3},... | collective-permute-start | bytes 196616 | tf_op jit(solution)/shard_map/ppermute | solution.py:112
  288.4 3.1 collective-permute-start.18
  294.3 2.4 collective-permute-start.22
  297.2 1.7 collective-permute-done.21
  299.9 4.3 %collective-permute-start.23 = (f32[512,2,128]{2,0,1:T(8,128)S(1)}, f32[512,2,128]{2,0,1:T(8,128)S(1)}, u32[]{:S(2)}, u32[]{:S(2)}) collective-permute-start(f32[512,2,128]{2,0,1:T(8,128)S(1)} %constant_dynamic-slice_fusion), channel_id=1, source_target_pairs={{0,0},{1,16},{2,32},{3,48},{4,64},{5,80},{6,96},{7,112},{8,1},{9,1... | collective-permute-start | bytes 1572872 | tf_op jit(solution)/shard_map/ppermute | solution.py:123
  304.4 46.4 %collective-permute-done.23 = f32[512,2,128]{2,0,1:T(8,128)S(1)} collective-permute-done((f32[512,2,128]{2,0,1:T(8,128)S(1)}, f32[512,2,128]{2,0,1:T(8,128)S(1)}, u32[]{:S(2)}, u32[]{:S(2)}) %collective-permute-start.23) | collective-permute-done | bytes 524320 | tf_op jit(solution)/shard_map/ppermute | solution.py:123
  350.7 1.8 fusion.35
  352.5 1.8 fusion.31
  354.3 2.0 fusion.19
  356.4 2.0 fusion.21
  358.4 2.5 pad_maximum_fusion
  (102 shorter events, 15.7 us)
Async XLA Ops:
  2.1 3.5 copy-start.1
  49.9 76.8 %all-to-all-start.1 = ((f32[16,128,4,8,9,2]{1,3,5,4,2,0:T(8,128)}), f32[16,128,4,8,9,2]{1,3,5,4,2,0:T(8,128)}, u32[]{:S(2)}, u32[]{:S(2)}) async-start(f32[16,128,4,8,9,2]{1,3,5,4,2,0:T(8,128)} %copy.55), calls=%async_computation.1 | async-start | bytes 9437184 | tf_op jit(solution)/shard_map/all_to_all | solution.py:82
  72.8 60.7 %copy-start.2 = (s32[8192]{0:T(1024)S(1)}, s32[8192]{0:T(1024)}, u32[]{:S(2)}) copy-start(s32[8192]{0:T(1024)} %param.18) | copy-start | bytes 98308
  126.7 74.1 %all-to-all-start = ((f32[16,128,4,8,9,2]{1,3,5,4,2,0:T(8,128)}), f32[16,128,4,8,9,2]{1,3,5,4,2,0:T(8,128)}, u32[]{:S(2)}, u32[]{:S(2)}) async-start(f32[16,128,4,8,9,2]{1,3,5,4,2,0:T(8,128)} %copy.53), calls=%async_computation | async-start | bytes 9437184 | tf_op jit(solution)/shard_map/all_to_all | solution.py:82
  239.8 7.6 %collective-permute-start.6 = (f32[128,2,128]{2,0,1:T(8,128)S(1)}, f32[128,2,128]{2,0,1:T(8,128)S(1)}, u32[]{:S(2)}, u32[]{:S(2)}) collective-permute-start(f32[128,2,128]{2,0,1:T(8,128)S(1)} %get-tuple-element.28), channel_id=1, source_target_pairs={{0,112},{16,0},{32,16},{48,32},{64,48},{80,64},{96,80},{112,96},{1... | collective-permute-start | bytes 393224 | tf_op jit(solution)/shard_map/ppermute | solution.py:104
  241.0 7.4 %collective-permute-start.5 = (f32[128,2,128]{2,0,1:T(8,128)S(1)}, f32[128,2,128]{2,0,1:T(8,128)S(1)}, u32[]{:S(2)}, u32[]{:S(2)}) collective-permute-start(f32[128,2,128]{2,0,1:T(8,128)S(1)} %get-tuple-element.29), channel_id=1, source_target_pairs={{0,96},{16,112},{32,0},{48,16},{64,32},{80,48},{96,64},{112,80},{1... | collective-permute-start | bytes 393224 | tf_op jit(solution)/shard_map/ppermute | solution.py:104
  244.0 5.9 %collective-permute-start.4 = (f32[128,2,128]{2,0,1:T(8,128)S(1)}, f32[128,2,128]{2,0,1:T(8,128)S(1)}, u32[]{:S(2)}, u32[]{:S(2)}) collective-permute-start(f32[128,2,128]{2,0,1:T(8,128)S(1)} %get-tuple-element.30), channel_id=1, source_target_pairs={{0,80},{16,96},{32,112},{48,0},{64,16},{80,32},{96,48},{112,64},{1... | collective-permute-start | bytes 393224 | tf_op jit(solution)/shard_map/ppermute | solution.py:104
  244.0 10.0 %collective-permute-start.3 = (f32[128,2,128]{2,0,1:T(8,128)S(1)}, f32[128,2,128]{2,0,1:T(8,128)S(1)}, u32[]{:S(2)}, u32[]{:S(2)}) collective-permute-start(f32[128,2,128]{2,0,1:T(8,128)S(1)} %get-tuple-element.31), channel_id=1, source_target_pairs={{0,64},{16,80},{32,96},{48,112},{64,0},{80,16},{96,32},{112,48},{1... | collective-permute-start | bytes 393224 | tf_op jit(solution)/shard_map/ppermute | solution.py:104
  247.5 7.4 %collective-permute-start.2 = (f32[128,2,128]{2,0,1:T(8,128)S(1)}, f32[128,2,128]{2,0,1:T(8,128)S(1)}, u32[]{:S(2)}, u32[]{:S(2)}) collective-permute-start(f32[128,2,128]{2,0,1:T(8,128)S(1)} %get-tuple-element.32), channel_id=1, source_target_pairs={{0,48},{16,64},{32,80},{48,96},{64,112},{80,0},{96,16},{112,32},{1... | collective-permute-start | bytes 393224 | tf_op jit(solution)/shard_map/ppermute | solution.py:104
  247.5 12.4 %collective-permute-start.1 = (f32[128,2,128]{2,0,1:T(8,128)S(1)}, f32[128,2,128]{2,0,1:T(8,128)S(1)}, u32[]{:S(2)}, u32[]{:S(2)}) collective-permute-start(f32[128,2,128]{2,0,1:T(8,128)S(1)} %get-tuple-element.33), channel_id=1, source_target_pairs={{0,32},{16,48},{32,64},{48,80},{64,96},{80,112},{96,0},{112,16},{1... | collective-permute-start | bytes 393224 | tf_op jit(solution)/shard_map/ppermute | solution.py:104
  248.4 11.5 %collective-permute-start = (f32[128,2,128]{2,0,1:T(8,128)S(1)}, f32[128,2,128]{2,0,1:T(8,128)S(1)}, u32[]{:S(2)}, u32[]{:S(2)}) collective-permute-start(f32[128,2,128]{2,0,1:T(8,128)S(1)} %get-tuple-element.27), channel_id=1, source_target_pairs={{0,16},{16,32},{32,48},{48,64},{64,80},{80,96},{96,112},{112,0},{1... | collective-permute-start | bytes 393224 | tf_op jit(solution)/shard_map/ppermute | solution.py:104
  260.0 8.9 %collective-permute-start.7 = (f32[64,2,128]{2,0,1:T(8,128)S(1)}, f32[64,2,128]{2,0,1:T(8,128)S(1)}, u32[]{:S(2)}, u32[]{:S(2)}) collective-permute-start(f32[64,2,128]{2,0,1:T(8,128)S(1)} %dynamic-slice_bitcast_fusion.7), channel_id=1, source_target_pairs={{0,15},{1,14},{2,13},{3,12},{4,11},{5,10},{6,9},{7,8},{8,7},{9,6},... | collective-permute-start | bytes 196616 | tf_op jit(solution)/shard_map/ppermute | solution.py:108
  269.0 8.6 %collective-permute-start.8 = (f32[64,2,128]{2,0,1:T(8,128)S(1)}, f32[64,2,128]{2,0,1:T(8,128)S(1)}, u32[]{:S(2)}, u32[]{:S(2)}) collective-permute-start(f32[64,2,128]{2,0,1:T(8,128)S(1)} %get-tuple-element.16), channel_id=1, source_target_pairs={{0,1},{1,2},{2,3},{3,4},{4,5},{5,6},{6,7},{7,8},{8,9},{9,10},{10,1... | collective-permute-start | bytes 196616 | tf_op jit(solution)/shard_map/ppermute | solution.py:112
  269.1 9.1 %collective-permute-start.9 = (f32[64,2,128]{2,0,1:T(8,128)S(1)}, f32[64,2,128]{2,0,1:T(8,128)S(1)}, u32[]{:S(2)}, u32[]{:S(2)}) collective-permute-start(f32[64,2,128]{2,0,1:T(8,128)S(1)} %get-tuple-element.16), channel_id=1, source_target_pairs={{0,2},{1,3},{2,4},{3,5},{4,6},{5,7},{6,8},{7,9},{8,10},{9,11},{10,... | collective-permute-start | bytes 196616 | tf_op jit(solution)/shard_map/ppermute | solution.py:112
  269.2 9.9 %collective-permute-start.10 = (f32[64,2,128]{2,0,1:T(8,128)S(1)}, f32[64,2,128]{2,0,1:T(8,128)S(1)}, u32[]{:S(2)}, u32[]{:S(2)}) collective-permute-start(f32[64,2,128]{2,0,1:T(8,128)S(1)} %get-tuple-element.16), channel_id=1, source_target_pairs={{0,3},{1,4},{2,5},{3,6},{4,7},{5,8},{6,9},{7,10},{8,11},{9,12},{10... | collective-permute-start | bytes 196616 | tf_op jit(solution)/shard_map/ppermute | solution.py:112
  271.1 11.7 %collective-permute-start.11 = (f32[64,2,128]{2,0,1:T(8,128)S(1)}, f32[64,2,128]{2,0,1:T(8,128)S(1)}, u32[]{:S(2)}, u32[]{:S(2)}) collective-permute-start(f32[64,2,128]{2,0,1:T(8,128)S(1)} %get-tuple-element.16), channel_id=1, source_target_pairs={{0,4},{1,5},{2,6},{3,7},{4,8},{5,9},{6,10},{7,11},{8,12},{9,13},{1... | collective-permute-start | bytes 196616 | tf_op jit(solution)/shard_map/ppermute | solution.py:112
  271.1 11.8 %collective-permute-start.12 = (f32[64,2,128]{2,0,1:T(8,128)S(1)}, f32[64,2,128]{2,0,1:T(8,128)S(1)}, u32[]{:S(2)}, u32[]{:S(2)}) collective-permute-start(f32[64,2,128]{2,0,1:T(8,128)S(1)} %get-tuple-element.16), channel_id=1, source_target_pairs={{0,5},{1,6},{2,7},{3,8},{4,9},{5,10},{6,11},{7,12},{8,13},{9,14},{... | collective-permute-start | bytes 196616 | tf_op jit(solution)/shard_map/ppermute | solution.py:112
  277.6 10.7 %collective-permute-start.13 = (f32[64,2,128]{2,0,1:T(8,128)S(1)}, f32[64,2,128]{2,0,1:T(8,128)S(1)}, u32[]{:S(2)}, u32[]{:S(2)}) collective-permute-start(f32[64,2,128]{2,0,1:T(8,128)S(1)} %get-tuple-element.16), channel_id=1, source_target_pairs={{0,6},{1,7},{2,8},{3,9},{4,10},{5,11},{6,12},{7,13},{8,14},{9,15},... | collective-permute-start | bytes 196616 | tf_op jit(solution)/shard_map/ppermute | solution.py:112
  278.2 13.2 %collective-permute-start.14 = (f32[64,2,128]{2,0,1:T(8,128)S(1)}, f32[64,2,128]{2,0,1:T(8,128)S(1)}, u32[]{:S(2)}, u32[]{:S(2)}) collective-permute-start(f32[64,2,128]{2,0,1:T(8,128)S(1)} %get-tuple-element.16), channel_id=1, source_target_pairs={{0,7},{1,8},{2,9},{3,10},{4,11},{5,12},{6,13},{7,14},{8,15},{9,0},... | collective-permute-start | bytes 196616 | tf_op jit(solution)/shard_map/ppermute | solution.py:112
  279.0 12.6 %collective-permute-start.15 = (f32[64,2,128]{2,0,1:T(8,128)S(1)}, f32[64,2,128]{2,0,1:T(8,128)S(1)}, u32[]{:S(2)}, u32[]{:S(2)}) collective-permute-start(f32[64,2,128]{2,0,1:T(8,128)S(1)} %get-tuple-element.16), channel_id=1, source_target_pairs={{0,8},{1,9},{2,10},{3,11},{4,12},{5,13},{6,14},{7,15},{8,0},{9,1},... | collective-permute-start | bytes 196616 | tf_op jit(solution)/shard_map/ppermute | solution.py:112
  282.8 10.2 %collective-permute-start.16 = (f32[64,2,128]{2,0,1:T(8,128)S(1)}, f32[64,2,128]{2,0,1:T(8,128)S(1)}, u32[]{:S(2)}, u32[]{:S(2)}) collective-permute-start(f32[64,2,128]{2,0,1:T(8,128)S(1)} %get-tuple-element.16), channel_id=1, source_target_pairs={{0,9},{1,10},{2,11},{3,12},{4,13},{5,14},{6,15},{7,0},{8,1},{9,2},... | collective-permute-start | bytes 196616 | tf_op jit(solution)/shard_map/ppermute | solution.py:112
  282.9 11.4 %collective-permute-start.17 = (f32[64,2,128]{2,0,1:T(8,128)S(1)}, f32[64,2,128]{2,0,1:T(8,128)S(1)}, u32[]{:S(2)}, u32[]{:S(2)}) collective-permute-start(f32[64,2,128]{2,0,1:T(8,128)S(1)} %get-tuple-element.16), channel_id=1, source_target_pairs={{0,10},{1,11},{2,12},{3,13},{4,14},{5,15},{6,0},{7,1},{8,2},{9,3},... | collective-permute-start | bytes 196616 | tf_op jit(solution)/shard_map/ppermute | solution.py:112
  288.4 8.3 %collective-permute-start.18 = (f32[64,2,128]{2,0,1:T(8,128)S(1)}, f32[64,2,128]{2,0,1:T(8,128)S(1)}, u32[]{:S(2)}, u32[]{:S(2)}) collective-permute-start(f32[64,2,128]{2,0,1:T(8,128)S(1)} %get-tuple-element.16), channel_id=1, source_target_pairs={{0,11},{1,12},{2,13},{3,14},{4,15},{5,0},{6,1},{7,2},{8,3},{9,4},{... | collective-permute-start | bytes 196616 | tf_op jit(solution)/shard_map/ppermute | solution.py:112
  291.4 5.5 %collective-permute-start.19 = (f32[64,2,128]{2,0,1:T(8,128)S(1)}, f32[64,2,128]{2,0,1:T(8,128)S(1)}, u32[]{:S(2)}, u32[]{:S(2)}) collective-permute-start(f32[64,2,128]{2,0,1:T(8,128)S(1)} %get-tuple-element.16), channel_id=1, source_target_pairs={{0,12},{1,13},{2,14},{3,15},{4,0},{5,1},{6,2},{7,3},{8,4},{9,5},{1... | collective-permute-start | bytes 196616 | tf_op jit(solution)/shard_map/ppermute | solution.py:112
  291.5 12.7 %copy-start.3 = (s32[128]{0:T(128)S(1)}, s32[128]{0:T(128)}, u32[]{:S(2)}) copy-start(s32[128]{0:T(128)} %param.17) | copy-start | bytes 1540
  291.6 12.7 %copy-start.4 = (s32[128]{0:T(128)S(1)}, s32[128]{0:T(128)}, u32[]{:S(2)}) copy-start(s32[128]{0:T(128)} %param.16) | copy-start | bytes 1540
  291.6 12.7 %copy-start.5 = (f32[64]{0:T(128)S(1)}, f32[64]{0:T(128)}, u32[]{:S(2)}) copy-start(f32[64]{0:T(128)} %param.14) | copy-start | bytes 772
  291.6 12.7 %copy-start.6 = (f32[64]{0:T(128)S(1)}, f32[64]{0:T(128)}, u32[]{:S(2)}) copy-start(f32[64]{0:T(128)} %param.15) | copy-start | bytes 772
  291.6 5.5 %collective-permute-start.20 = (f32[64,2,128]{2,0,1:T(8,128)S(1)}, f32[64,2,128]{2,0,1:T(8,128)S(1)}, u32[]{:S(2)}, u32[]{:S(2)}) collective-permute-start(f32[64,2,128]{2,0,1:T(8,128)S(1)} %get-tuple-element.16), channel_id=1, source_target_pairs={{0,13},{1,14},{2,15},{3,0},{4,1},{5,2},{6,3},{7,4},{8,5},{9,6},{10... | collective-permute-start | bytes 196616 | tf_op jit(solution)/shard_map/ppermute | solution.py:112
  293.1 5.8 %collective-permute-start.21 = (f32[64,2,128]{2,0,1:T(8,128)S(1)}, f32[64,2,128]{2,0,1:T(8,128)S(1)}, u32[]{:S(2)}, u32[]{:S(2)}) collective-permute-start(f32[64,2,128]{2,0,1:T(8,128)S(1)} %get-tuple-element.16), channel_id=1, source_target_pairs={{0,14},{1,15},{2,0},{3,1},{4,2},{5,3},{6,4},{7,5},{8,6},{9,7},{10,... | collective-permute-start | bytes 196616 | tf_op jit(solution)/shard_map/ppermute | solution.py:112
  294.3 4.6 %collective-permute-start.22 = (f32[64,2,128]{2,0,1:T(8,128)S(1)}, f32[64,2,128]{2,0,1:T(8,128)S(1)}, u32[]{:S(2)}, u32[]{:S(2)}) collective-permute-start(f32[64,2,128]{2,0,1:T(8,128)S(1)} %get-tuple-element.16), channel_id=1, source_target_pairs={{0,15},{1,0},{2,1},{3,2},{4,3},{5,4},{6,5},{7,6},{8,7},{9,8},{10,9... | collective-permute-start | bytes 196616 | tf_op jit(solution)/shard_map/ppermute | solution.py:112
  299.6 54.7 %copy-start = (f32[2,1024,512]{2,1,0:T(8,128)S(1)}, f32[2,1024,512]{2,1,0:T(8,128)}, u32[]{:S(2)}) copy-start(f32[2,1024,512]{2,1,0:T(8,128)} %param.19) | copy-start | bytes 12582916
  299.9 50.8 %collective-permute-start.23 = (f32[512,2,128]{2,0,1:T(8,128)S(1)}, f32[512,2,128]{2,0,1:T(8,128)S(1)}, u32[]{:S(2)}, u32[]{:S(2)}) collective-permute-start(f32[512,2,128]{2,0,1:T(8,128)S(1)} %constant_dynamic-slice_fusion), channel_id=1, source_target_pairs={{0,0},{1,16},{2,32},{3,48},{4,64},{5,80},{6,96},{7,112},{8,1},{9,1... | collective-permute-start | bytes 1572872 | tf_op jit(solution)/shard_map/ppermute | solution.py:123
